TPU v7x, 128 devices: a whole 4x4x4 slice. The times are simulated.
128 devices in a mesh: group: 8 (over y_lo, x), head: 16 (over y_hi, z, core).
Axes of the slice: x: 4, y: 4 (y_hi: 2, y_lo: 2; y = y_hi * 2 + y_lo), z: 4, core: 2. Of those that a mesh axis runs over, the one named last changes fastest.
Arguments:
- symbol_lookup_table: bfloat16 [65536, 2048], P(None, 'head'), may hold values from -6 to 6
- joined_linear_maps: float32 [5, 2048, 2048], P(None, 'group', 'head'), may hold values from -0.125 to 0.125
- feedforward_lookup_map: float32 [2048, 7168], P('group', 'head'), may hold values from -0.125 to 0.125
- timeblend_result_map: float32 [2048, 2048], P('head', 'group'), may hold values from -0.125 to 0.125
- feedforward_content_map: float32 [7168, 2048], P('head', 'group'), may hold values from -0.0625 to 0.0625
- lag_blend_coefs: float32 [8, 2048], replicated, may hold values from 0 to 1
- blend_narrowing_map: bfloat16 [2048, 160], replicated, may hold values from -0.125 to 0.125
- blend_widening_maps: bfloat16 [5, 32, 2048], replicated, may hold values from -0.59765625 to 0.59765625
- fading_narrowing_map: bfloat16 [2048, 64], replicated, may hold values from -0.125 to 0.125
- fading_widening_map: bfloat16 [64, 2048], P(None, 'head'), as said below
- initial_fading_power: float32 [2048], P('head'), may hold values from -12 to -2.9
- present_symbol_extra: float32 [2048], P('head'), may hold values from -3 to 3
- attender_scaling_coefs: float32 [2048], P('head'), may hold values from 0.5 to 2
- active_cluster_sheets: int32 [8], replicated, may hold values from 2 to 4, as said below
- sheets_for_inquiry: int32 [7], replicated, may hold values from 2 to 7, as said below
- sheet_symbol_indices: int32 [24, 256], replicated, may hold values from 0 to 65535
Outputs:
- hidden_states: bfloat16 [8192, 2048], P('group', 'head')
- page_states: float32 [32, 32, 4096], P('group', 'head')
- shift_edges: float32 [32, 2, 2048], P('group', None, 'head')
Inputs may be any that keep to these rules, and one draw needn't show every extreme that they name: `active_cluster_sheets`: they sum to 24; the two groups at one end of the axis, the first two or the last two, hold 4 pages each. `sheets_for_inquiry`: they sum to 24; the first page of every group but group 0 continues a request; the first or the last request holds 7 pages. `fading_widening_map`: each entry lies within 2.5 / sqrt(64) of zero.
All inputs are finite; a program needn't handle non-finite values.
Results may differ from a plain program's by a relative error of at most 0.017.
Values may be sent and summed in bfloat16 or wider, within the bound.
No kernel may reach another device: no remote copies, remote signals or barrier semaphores. Data moves between devices by JAX's collectives and lax.ppermute only.
A program may use at most 192 MiB of HBM per device.

v0:
```python
import jax
import jax.numpy as jnp
from jax import lax
from jax.sharding import PartitionSpec as P

ATTENTION_DEPTH = 64
PAGE = 256
SLOTS = 4
BLOCK = 128
EXACT_ARITHMETIC = lax.Precision.HIGHEST
LAYER_EPS = 1e-05
GROUP_EPS = 0.00064


def passed_along(value, axis, steps):
    count = lax.axis_size(axis)
    initial, last = (max(0, -steps), min(count, count - steps))
    return lax.ppermute(value, axis, [(source, source + steps) for source in range(initial, last)])


def layer_norm(value_rows):
    value_rows = value_rows.astype(jnp.float32)
    centered = value_rows - jnp.mean(value_rows, axis=-1, keepdims=True)
    return centered * lax.rsqrt(jnp.mean(centered * centered, axis=-1, keepdims=True) + LAYER_EPS)


def mixed_inputs(current, previous, lag_blend_coefs, blend_narrowing_map, blend_widening_maps):
    delta_rows = previous - current
    seeded = (current + delta_rows * lag_blend_coefs[0]).astype(jnp.bfloat16)
    low_rank = jnp.tanh(
        jnp.dot(seeded, blend_narrowing_map, preferred_element_type=jnp.float32)
    ).astype(jnp.bfloat16)
    rank_width = blend_widening_maps.shape[1]
    result_lines = []
    for number in range(5):
        column_part = low_rank[:, number * rank_width : (number + 1) * rank_width]
        offset = jnp.dot(
            column_part, blend_widening_maps[number], preferred_element_type=jnp.float32
        )
        result_lines.append(
            (current + delta_rows * (lag_blend_coefs[number + 1] + offset)).astype(jnp.bfloat16)
        )
    return result_lines


def log_decay(mixed_decay, fading_narrowing_map, fading_widening_map, initial_fading_power):
    hidden_low = jnp.tanh(
        jnp.dot(mixed_decay, fading_narrowing_map, preferred_element_type=jnp.float32)
    ).astype(jnp.bfloat16)
    return -jnp.exp(
        initial_fading_power
        + jnp.dot(hidden_low, fading_widening_map, preferred_element_type=jnp.float32)
    )


def group_norm(value_rows):
    shaped = value_rows.reshape(value_rows.shape[0], -1, ATTENTION_DEPTH)
    centered = shaped - jnp.mean(shaped, axis=-1, keepdims=True)
    normed = centered * lax.rsqrt(jnp.mean(centered * centered, axis=-1, keepdims=True) + GROUP_EPS)
    return normed.reshape(value_rows.shape)


def per_device(
    symbol_lookup_table,
    joined_linear_maps,
    feedforward_lookup_map,
    timeblend_result_map,
    feedforward_content_map,
    lag_blend_coefs,
    blend_narrowing_map,
    blend_widening_maps,
    fading_narrowing_map,
    fading_widening_map,
    initial_fading_power,
    present_symbol_extra,
    attender_scaling_coefs,
    active_cluster_sheets,
    sheets_for_inquiry,
    sheet_symbol_indices,
):
    group_count = lax.axis_size("group")
    group_here = lax.axis_index("group")
    head_here = lax.axis_index("head")
    features_on_shard = present_symbol_extra.shape[0]
    attenders_on_shard = features_on_shard // ATTENTION_DEPTH
    slot_rows = SLOTS * PAGE
    full_width = lag_blend_coefs.shape[1]
    group_number = jnp.arange(group_count, dtype=jnp.int32)
    pick_group = group_number == group_here
    live_count = jnp.sum(jnp.where(pick_group, active_cluster_sheets, 0))
    group_first = jnp.cumsum(active_cluster_sheets) - active_cluster_sheets
    first_page = jnp.sum(jnp.where(pick_group, group_first, 0))
    slot_number = jnp.arange(SLOTS, dtype=jnp.int32)
    slot_live = slot_number < live_count
    request_first = jnp.cumsum(sheets_for_inquiry) - sheets_for_inquiry
    page_here = first_page + slot_number
    begins = jnp.any(page_here[:, None] == request_first[None, :], axis=1)
    continues = jnp.where(slot_live & jnp.logical_not(begins), 1.0, 0.0).astype(jnp.float32)
    safe_page = jnp.where(slot_live, page_here, 0)
    tokens_here = jnp.take(sheet_symbol_indices, safe_page, axis=0)
    before_token = jnp.take(sheet_symbol_indices[:, -1], jnp.maximum(safe_page - 1, 0))
    edge_pad = jnp.concatenate([before_token, jnp.zeros((8 - SLOTS,), before_token.dtype)])
    all_tokens = jnp.concatenate([tokens_here.reshape(-1), edge_pad])
    own_rows = jnp.take(symbol_lookup_table, all_tokens, axis=0)
    gathered_rows = lax.all_gather(own_rows, "head", axis=1, tiled=True)
    embedded = gathered_rows[:slot_rows]
    edge_rows = gathered_rows[slot_rows : slot_rows + SLOTS]
    map_count = joined_linear_maps.shape[0]
    first_pack = jnp.concatenate([joined_linear_maps, timeblend_result_map.T[None]], axis=0).astype(
        jnp.bfloat16
    )
    second_pack = jnp.stack([feedforward_lookup_map, feedforward_content_map.T], axis=0).astype(
        jnp.bfloat16
    )
    first_full = lax.all_gather(first_pack, "group", axis=1, tiled=True)
    second_full = lax.all_gather(second_pack, "group", axis=1, tiled=True)
    projections = first_full[:map_count]
    output_weight_t = first_full[map_count]
    key_weight = second_full[0]
    value_weight_t = second_full[1]
    current = layer_norm(embedded)
    edge_first = layer_norm(edge_rows) * continues[:, None]
    current_pages = current.reshape(SLOTS, PAGE, full_width)
    previous = jnp.concatenate([edge_first[:, None, :], current_pages[:, :-1, :]], axis=1).reshape(
        slot_rows, full_width
    )
    mixed_decay, mixed_key, mixed_value, mixed_query, mixed_gate = mixed_inputs(
        current, previous, lag_blend_coefs, blend_narrowing_map, blend_widening_maps
    )
    fading_multipliers = log_decay(
        mixed_decay, fading_narrowing_map, fading_widening_map, initial_fading_power
    )
    acceptance_lines = jnp.dot(mixed_query, projections[0], preferred_element_type=jnp.float32)
    present_lookups = jnp.dot(mixed_key, projections[1], preferred_element_type=jnp.float32)
    present_contents = jnp.dot(mixed_value, projections[2], preferred_element_type=jnp.float32)
    gate_raw = jnp.dot(mixed_gate, projections[3], preferred_element_type=jnp.float32)
    gating = jax.nn.silu(gate_raw)
    blocks = slot_rows // BLOCK
    per_page = PAGE // BLOCK

    def to_blocks(value_rows):
        return value_rows.reshape(blocks, BLOCK, attenders_on_shard, ATTENTION_DEPTH).transpose(
            0, 2, 1, 3
        )

    block_index = jnp.arange(blocks, dtype=jnp.int32)
    block_start = block_index % per_page == 0
    block_slot = block_index // per_page
    slot_keep = continues * (slot_number > 0)
    keep_state = jnp.where(block_start, jnp.take(slot_keep, block_slot), 1.0)
    keep_factor = jnp.where(block_start, jnp.take(continues, block_slot), 1.0)
    attender_extra = present_symbol_extra.reshape(attenders_on_shard, ATTENTION_DEPTH)
    strictly_lower = jnp.arange(BLOCK)[:, None] > jnp.arange(BLOCK)[None, :]
    askers_b = to_blocks(acceptance_lines)
    lookups_b = to_blocks(present_lookups)
    values_b = to_blocks(present_contents)
    decay_b = to_blocks(fading_multipliers)
    inclusive = jnp.cumsum(decay_b, axis=2)
    exclusive = inclusive - decay_b
    query_scaled = askers_b * jnp.exp(exclusive)
    key_scaled = lookups_b * jnp.exp(-inclusive)
    scores = jnp.einsum("bhts,bhus->bhtu", query_scaled, key_scaled, precision=EXACT_ARITHMETIC)
    scores = jnp.where(strictly_lower, scores, 0.0)
    selfpair_contribution = jnp.sum(askers_b * attender_extra[None, :, None, :] * lookups_b, axis=3)
    intra = (
        jnp.einsum("bhtu,bhuj->bhtj", scores, values_b, precision=EXACT_ARITHMETIC)
        + selfpair_contribution[..., None] * values_b
    )
    block_total = inclusive[:, :, -1, :]
    block_decay = jnp.exp(block_total)
    key_end = lookups_b * jnp.exp(block_total[:, :, None, :] - inclusive)
    block_kv = jnp.einsum("bhts,bhtj->bhsj", key_end, values_b, precision=EXACT_ARITHMETIC)
    sweep = jnp.zeros((attenders_on_shard, ATTENTION_DEPTH, ATTENTION_DEPTH), jnp.float32)
    factor = jnp.ones((attenders_on_shard, ATTENTION_DEPTH), jnp.float32)
    starts, factors_before, ends, factors_after = ([], [], [], [])
    for number in range(blocks):
        sweep = sweep * keep_state[number]
        factor = factor * keep_factor[number]
        starts.append(sweep)
        factors_before.append(factor)
        sweep = block_decay[number][:, :, None] * sweep + block_kv[number]
        factor = factor * block_decay[number]
        ends.append(sweep)
        factors_after.append(factor)
    block_out = intra + jnp.einsum(
        "bhts,bhsj->bhtj", query_scaled, jnp.stack(starts), precision=EXACT_ARITHMETIC
    )
    carry_rows = query_scaled * jnp.stack(factors_before)[:, :, None, :]
    block_states = jnp.stack(ends)
    block_factors = jnp.stack(factors_after)
    page_end = block_states[per_page - 1 :: per_page]
    page_factor = block_factors[per_page - 1 :: per_page]
    last_pick = (slot_number == live_count - 1).astype(jnp.float32)
    leaving_state = jnp.einsum("s,shij->hij", last_pick, page_end, precision=EXACT_ARITHMETIC)
    leaving_factor = jnp.einsum("s,shi->hi", last_pick, page_factor, precision=EXACT_ARITHMETIC)
    leaving_pack = jnp.concatenate([leaving_state, leaving_factor[:, None, :]], axis=1)
    every_pack = lax.all_gather(leaving_pack, "group", axis=0, tiled=False)
    incoming = jnp.zeros_like(leaving_state)
    for number in range(group_count - 1):
        composed = (
            every_pack[number, :, ATTENTION_DEPTH, :][:, :, None] * incoming
            + every_pack[number, :, :ATTENTION_DEPTH, :]
        )
        incoming = jnp.where(number < group_here, composed, incoming)
    block_out = block_out + jnp.einsum(
        "bhts,hsj->bhtj", carry_rows, incoming, precision=EXACT_ARITHMETIC
    )
    page_end = page_end + page_factor[:, :, :, None] * incoming[None]
    attended = block_out.transpose(0, 2, 1, 3).reshape(slot_rows, features_on_shard)
    normed = (group_norm(attended) * attender_scaling_coefs * gating).astype(jnp.bfloat16)
    mixer_total = lax.psum(
        lax.dot_general(
            normed, output_weight_t, (((1,), (1,)), ((), ())), preferred_element_type=jnp.float32
        ).astype(jnp.bfloat16),
        "head",
    ).astype(jnp.float32)
    residual = (embedded.astype(jnp.float32) + mixer_total).astype(jnp.bfloat16)
    last_residual = lax.dynamic_slice_in_dim(residual, live_count * PAGE - 1, 1, 0)
    arriving = passed_along(last_residual, "group", 1)
    channel_in = layer_norm(residual)
    channel_pages = channel_in.reshape(SLOTS, PAGE, full_width)
    edge_two = (
        jnp.concatenate([layer_norm(arriving), channel_pages[:-1, -1, :]], axis=0)
        * continues[:, None]
    )
    channel_prev = jnp.concatenate(
        [edge_two[:, None, :], channel_pages[:, :-1, :]], axis=1
    ).reshape(slot_rows, full_width)
    channel_delta = channel_prev - channel_in
    key_input = (channel_in + channel_delta * lag_blend_coefs[6]).astype(jnp.bfloat16)
    gate_input = (channel_in + channel_delta * lag_blend_coefs[7]).astype(jnp.bfloat16)
    gate_raw_two = jnp.dot(gate_input, projections[4], preferred_element_type=jnp.float32)
    key_raw = jnp.dot(key_input, key_weight, preferred_element_type=jnp.float32)
    squared = jnp.square(jax.nn.relu(key_raw)).astype(jnp.bfloat16)
    channel = lax.psum_scatter(
        lax.dot_general(
            squared, value_weight_t, (((1,), (1,)), ((), ())), preferred_element_type=jnp.float32
        ).astype(jnp.bfloat16),
        "head",
        scatter_dimension=1,
        tiled=True,
    ).astype(jnp.float32)
    gate_two = jax.nn.sigmoid(gate_raw_two)
    residual_local = lax.dynamic_slice_in_dim(
        residual, head_here * features_on_shard, features_on_shard, 1
    )
    hidden = (residual_local.astype(jnp.float32) + gate_two * channel).astype(jnp.bfloat16)
    row_live = jnp.repeat(slot_live, PAGE)
    hidden_out = jnp.where(row_live[:, None], hidden, jnp.zeros_like(hidden))
    state_out = page_end.reshape(SLOTS, attenders_on_shard, ATTENTION_DEPTH * ATTENTION_DEPTH)
    state_out = jnp.where(slot_live[:, None, None], state_out, jnp.zeros_like(state_out))
    first_edge = lax.dynamic_slice_in_dim(
        current_pages[:, -1, :], head_here * features_on_shard, features_on_shard, 1
    )
    second_edge = lax.dynamic_slice_in_dim(
        channel_pages[:, -1, :], head_here * features_on_shard, features_on_shard, 1
    )
    edge_out = jnp.stack([first_edge, second_edge], axis=1)
    edge_out = jnp.where(slot_live[:, None, None], edge_out, jnp.zeros_like(edge_out))
    return (hidden_out, state_out, edge_out)


def solution(mesh):
    in_specs = (
        P(None, "head"),
        P(None, "group", "head"),
        P("group", "head"),
        P("head", "group"),
        P("head", "group"),
        P(),
        P(),
        P(),
        P(),
        P(None, "head"),
        P("head"),
        P("head"),
        P("head"),
        P(),
        P(),
        P(),
    )
    out_specs = (P("group", "head"), P("group", "head", None), P("group", None, "head"))
    return jax.shard_map(
        per_device, mesh=mesh, in_specs=in_specs, out_specs=out_specs, check_vma=False
    )
```

profile of v0, /device:TPU:0, one launch (start us, length us, event | category | flops | bytes accessed | tf_op | source)
XLA Modules:
  0.0 557.0 jit_solution(13444309957814497587)
XLA Ops:
  8.3 1.1 convert.17
  11.2 1.3 fusion.130
  12.5 1.3 fusion.132
  13.8 1.3 gather_fusion
  15.1 1.3 compare_and_fusion.2
  16.5 1.3 maximum_bitcast_fusion
  19.3 1.3 fusion.168
  20.8 10.5 %gather_fusion.2 = bf16[1032,128]{1,0:T(8,128)(2,1)S(1)} fusion(bf16[65536,128]{1,0:T(8,128)(2,1)} %param.18, s32[2048]{0:T(1024)S(1)} %pad_clamp_fusion), kind=kCustom, calls=%fused_computation.4 | custom fusion | bytes 532512 | tf_op jit(solution)/shard_map/jit(_take)/gather | solution.py:104
  31.3 1.3 compare_select_fusion.6
  42.2 1.3 fusion.146
  43.5 13.4 %all-gather.7.cloned.1.call-done = bf16[6,2048,128]{2,1,0:T(8,128)(2,1)} async-done(((bf16[6,256,128]{2,1,0:T(8,128)(2,1)}), bf16[6,2048,128]{2,1,0:T(8,128)(2,1)}) %all-gather.7.cloned.1.call-update) | async-done | bytes 3145744 | tf_op jit(solution)/shard_map/all_gather | solution.py:115
  56.9 1.5 slice_bitcast_fusion.15
  61.4 54.3 %all-gather.5.cloned.1.call-done = bf16[1032,2048]{1,0:T(8,128)(2,1)} async-done(((bf16[1032,128]{1,0:T(8,128)(2,1)}), bf16[1032,2048]{1,0:T(8,128)(2,1)}) %all-gather.5.cloned.1.call-update) | async-done | bytes 4227088 | tf_op jit(solution)/shard_map/all_gather | solution.py:105
  115.7 1.0 convert_reduce_fusion.2
  116.8 1.2 fusion.105
  118.0 2.8 convert_reduce_fusion
  120.8 3.1 fusion.4
  124.0 1.2 fusion.2
  125.3 4.7 pad_maximum_fusion
  131.0 4.2 bitcast_subtract_fusion.1
  135.2 2.7 fusion.22
  138.4 8.1 %fusion.29 = bf16[1024,64]{0,1:T(8,128)(2,1)S(1)} fusion(bf16[2048,64]{0,1:T(8,128)(2,1)S(1)} %copy-done.18, f32[1024,2048]{1,0:T(8,128)} %copy-done.2, f32[2048]{0:T(1024)S(1)} %bitcast.330, f32[1024]{0:T(1024)S(1)} %add_rsqrt_fusion.1, f32[1024]{0:T(1024)S(1)} %broadcast_multiply_fusion.2, bf16[5,32,2048]{2,1,0:T(8,128)(2,1)} %param.25, ...), kind=kOutput, calls=%fused_computation.63 | convolution fusion | flops 417398784 | bytes 13189120 | tf_op jit(solution)/shard_map/dot_general | solution.py:48
  149.2 5.0 slice_multiply_fusion.2
  155.0 6.8 %add_convert_fusion.3 = bf16[1024,2048]{1,0:T(8,128)(2,1)S(1)} fusion(f32[1024,2048]{1,0:T(8,128)} %copy-done.2, f32[2048]{0:T(1024)S(1)} %bitcast.323, f32[1024]{0:T(1024)S(1)} %add_rsqrt_fusion.1, f32[1024]{0:T(1024)S(1)} %broadcast_multiply_fusion.2, bf16[5,32,2048]{2,1,0:T(8,128)(2,1)} %param.25, bf16[1024,160]{0,1:T(8,128)(2,1)} %copy-done.15, ...), kind=kOutput, calls=%fused_computation.24 | convolution fusion | flops 148897792 | bytes 16990208 | tf_op jit(solution)/shard_map/dot_general | solution.py:37
  161.8 1.5 fusion.151
  163.4 7.5 %add_convert_fusion.6 = bf16[1024,2048]{1,0:T(8,128)(2,1)S(1)} fusion(f32[1024,2048]{1,0:T(8,128)} %copy-done.2, f32[2048]{0:T(1024)S(1)} %bitcast.322, f32[1024]{0:T(1024)S(1)} %add_rsqrt_fusion.1, f32[1024]{0:T(1024)S(1)} %broadcast_multiply_fusion.2, bf16[5,32,2048]{2,1,0:T(8,128)(2,1)} %param.25, bf16[1024,160]{0,1:T(8,128)(2,1)} %copy-done.15, ...), kind=kOutput, calls=%fused_computation.27 | convolution fusion | flops 148897792 | bytes 16990208 | tf_op jit(solution)/shard_map/dot_general | solution.py:37
  170.9 1.5 convolution_bitcast_fusion.4
  172.5 3.3 add_convert_fusion.4
  175.8 1.5 multiply_reduce_fusion.1
  177.4 1.1 fusion.34
  178.5 2.2 convolution_select_fusion
  187.9 29.0 %all-gather = f32[16,65,64]{1,2,0:T(8,128)S(1)} all-gather(f32[2,65,64]{1,2,0:T(8,128)S(1)} %pad_maximum_fusion.4), channel_id=2, replica_groups=mesh['group'=8,'head'=16] {'group'}, dimensions={0}, use_global_device_ids=true | all-gather | bytes 299520 | tf_op jit(solution)/shard_map/all_gather | solution.py:197
  217.3 2.1 fusion.18
  222.0 7.5 %multiply_convert_fusion.1 = bf16[1024,128]{1,0:T(8,128)(2,1)S(1)} fusion(bf16[6,2048,128]{2,1,0:T(8,128)(2,1)} %all-gather.7.cloned.1.call-done, f32[1024,2048]{1,0:T(8,128)} %copy-done.2, f32[2048]{0:T(1024)S(1)} %bitcast.329, f32[1024]{0:T(1024)S(1)} %add_rsqrt_fusion.1, f32[1024]{0:T(1024)S(1)} %broadcast_multiply_fusion.2, f32[1024,128]{1,0:T(8,128)S(1)} %copy.137, ...), kind=kOutput, calls=%fused_computation.81 | convolution fusion | flops 686948352 | bytes 15155712 | tf_op jit(solution)/shard_map/dot_general | solution.py:136
  229.5 4.3 convolution_convert_fusion.1
  235.6 146.8 %all-reduce.2.cloned.1.call-done = bf16[1024,2048]{1,0:T(8,128)(2,1)} async-done(((bf16[1024,2048]{1,0:T(8,128)(2,1)}), bf16[1024,2048]{1,0:T(8,128)(2,1)}) %all-reduce.2.cloned.1.call-update) | async-done | bytes 4194320 | tf_op jit(solution)/shard_map/psum | solution.py:211
  382.4 4.2 convert_reduce_fusion.1
  386.6 3.5 collective-permute-start
  390.1 1.2 fusion.5
  392.3 3.2 copy-done.5
  398.3 4.6 pad_maximum_fusion.1
  402.9 4.5 bitcast_subtract_fusion
  407.4 33.2 %all-gather.9.cloned.1.call-done = bf16[2,2048,448]{1,2,0:T(8,128)(2,1)} async-done(((bf16[2,256,448]{1,2,0:T(8,128)(2,1)}), bf16[2,2048,448]{1,2,0:T(8,128)(2,1)}) %all-gather.9.cloned.1.call-update) | async-done | bytes 3670032 | tf_op jit(solution)/shard_map/all_gather | solution.py:116
  440.6 12.2 %convolution_convert_fusion = bf16[1024,2048]{1,0:T(8,128)(2,1)} fusion(bf16[2,2048,448]{1,2,0:T(8,128)(2,1)} %all-gather.9.cloned.1.call-done, f32[1024,2048]{1,0:T(8,128)} %bitcast_subtract_fusion, f32[2048]{0:T(1024)S(1)} %bitcast.328, bf16[1024,2048]{1,0:T(8,128)(2,1)} %copy-done.3, f32[1024]{0:T(1024)S(1)} %add_rsqrt_fusion, ...), kind=kOutput, calls=%fused_computation.34 | convolution fusion | flops 3774152704 | bytes 20463616 | tf_op jit(solution)/shard_map/dot_general | solution.py:236
  452.8 6.5 %copy.152 = bf16[1024,2048]{0,1:T(8,128)(2,1)} copy(bf16[1024,2048]{1,0:T(8,128)(2,1)} %convolution_convert_fusion) | data formatting | bytes 8388608
  464.0 77.8 %reduce-scatter.4.cloned.1.call-done = bf16[128,1024]{1,0:T(8,128)(2,1)} async-done(((bf16[2048,1024]{1,0:T(8,128)(2,1)}), bf16[128,1024]{1,0:T(8,128)(2,1)}) %reduce-scatter.4.cloned.1.call-update) | async-done | bytes 262160
  541.8 1.2 copy.153
  543.0 7.3 %fusion.30 = bf16[1024,128]{1,0:T(8,128)(2,1)} fusion(f32[1024,2048]{1,0:T(8,128)} %bitcast_subtract_fusion, f32[2048]{0:T(1024)S(1)} %bitcast.327, bf16[6,2048,128]{2,1,0:T(8,128)(2,1)} %all-gather.7.cloned.1.call-done, bf16[1024,128]{1,0:T(8,128)(2,1)S(1)} %copy.153, bf16[1024,2048]{1,0:T(8,128)(2,1)} %copy-done.3, s32[]{:T(128)S(6)} %select_n.286, ...), kind=kOutput, calls=%fused_computation.65 | convolution fusion | flops 550633472 | bytes 13911044 | tf_op jit(solution)/shard_map/dot_general | solution.py:232
  (172 shorter events, 39.0 us)
Async XLA Ops:
  7.2 128.0 %copy-start = (bf16[2048,160]{0,1:T(8,128)(2,1)S(1)}, bf16[2048,160]{0,1:T(8,128)(2,1)}, u32[]{:S(2)}) copy-start(bf16[2048,160]{0,1:T(8,128)(2,1)} %param.24) | copy-start | bytes 1966084
  7.2 49.7 %all-gather.7.cloned.1.call-start = ((), (), s32[]{:S(2)}) async-start(), calls=%async_computation.2 | async-start | bytes 3538944 | tf_op jit(solution)/shard_map/all_gather | solution.py:115
  10.3 105.4 %all-gather.5.cloned.1.call-start = ((), (), s32[]{:S(2)}) async-start(), calls=%async_computation.1 | async-start | bytes 4491264 | tf_op jit(solution)/shard_map/all_gather | solution.py:105
  33.6 348.7 %all-reduce.2.cloned.1.call-start = ((), (), s32[]{:S(2)}) async-start(), calls=%async_computation.3 | async-start | bytes 8388608 | tf_op jit(solution)/shard_map/psum | solution.py:211
  115.7 8.2 %slice-start = ((s8[4227072]{0:T(1024)(128)(4,1)}), s8[4194304]{0:T(1024)(128)(4,1)S(1)}, s32[]{:S(2)}) async-start(s8[4227072]{0:T(1024)(128)(4,1)} %bitcast.296), calls=%async_computation.6 | async-start | bytes 8388608
  118.0 5.9 %slice-start.1 = ((s8[4227072]{0:T(1024)(128)(4,1)}), s8[32768]{0:T(1024)(128)(4,1)S(1)}, s32[]{:S(2)}) async-start(s8[4227072]{0:T(1024)(128)(4,1)} %bitcast.296), calls=%async_computation.7 | async-start | bytes 65536
  125.2 5.7 %copy-start.6 = (f32[1024,2048]{1,0:T(8,128)}, f32[1024,2048]{1,0:T(8,128)S(1)}, u32[]{:S(2)}) copy-start(f32[1024,2048]{1,0:T(8,128)S(1)} %fusion.2) | copy-start | bytes 25165828
  135.2 3.2 copy-start.2
  135.2 3.2 copy-start.18
  138.4 8.1 %copy-start.15 = (bf16[1024,160]{0,1:T(8,128)(2,1)}, bf16[1024,160]{0,1:T(8,128)(2,1)S(1)}, u32[]{:S(2)}) copy-start(bf16[1024,160]{0,1:T(8,128)(2,1)S(1)} %fusion.22) | copy-start | bytes 983044
  138.4 8.1 %copy-start.16 = (bf16[64,128]{1,0:T(8,128)(2,1)S(1)}, bf16[64,128]{1,0:T(8,128)(2,1)}, u32[]{:S(2)}) copy-start(bf16[64,128]{1,0:T(8,128)(2,1)} %param.27) | copy-start | bytes 49156
  138.4 8.1 %copy-start.17 = (f32[128]{0:T(128)S(1)}, f32[128]{0:T(128)}, u32[]{:S(2)}) copy-start(f32[128]{0:T(128)} %param.28) | copy-start | bytes 1540
  155.0 6.8 %copy-start.9 = (bf16[128,2048]{1,0:T(8,128)(2,1)S(1)}, bf16[128,2048]{1,0:T(8,128)(2,1)}, u32[]{:S(2)}) copy-start(bf16[128,2048]{1,0:T(8,128)(2,1)} %copy.128) | copy-start | bytes 1572868
  161.8 10.7 %slice-start.2 = ((s8[4227072]{0:T(1024)(128)(4,1)}), s8[4194304]{0:T(1024)(128)(4,1)S(1)}, s32[]{:S(2)}) async-start(s8[4227072]{0:T(1024)(128)(4,1)} %bitcast.298), calls=%async_computation.8 | async-start | bytes 8388608
  161.8 10.7 %slice-start.4 = ((s8[8388608]{0:T(1024)(128)(4,1)}), s8[4194304]{0:T(1024)(128)(4,1)S(1)}, s32[]{:S(2)}) async-start(s8[8388608]{0:T(1024)(128)(4,1)} %bitcast.300), calls=%async_computation.10 | async-start | bytes 8388608
  163.4 7.6 %copy-start.8 = (bf16[128,2048]{1,0:T(8,128)(2,1)S(1)}, bf16[128,2048]{1,0:T(8,128)(2,1)}, u32[]{:S(2)}) copy-start(bf16[128,2048]{1,0:T(8,128)(2,1)} %copy.121) | copy-start | bytes 1572868
  163.4 9.1 %slice-start.3 = ((s8[4227072]{0:T(1024)(128)(4,1)}), s8[32768]{0:T(1024)(128)(4,1)S(1)}, s32[]{:S(2)}) async-start(s8[4227072]{0:T(1024)(128)(4,1)} %bitcast.298), calls=%async_computation.9 | async-start | bytes 65536
  163.4 9.1 %slice-start.5 = ((s8[8388608]{0:T(1024)(128)(4,1)}), s8[4194304]{0:T(1024)(128)(4,1)S(1)}, s32[]{:S(2)}) async-start(s8[8388608]{0:T(1024)(128)(4,1)} %bitcast.300), calls=%async_computation.11 | async-start | bytes 8388608
  172.5 3.3 copy-start.7
  175.8 4.9 copy-start.12
  182.3 39.8 %copy-start.19 = (f32[128]{0:T(128)S(1)}, f32[128]{0:T(128)}, u32[]{:S(2)}) copy-start(f32[128]{0:T(128)} %param.30) | copy-start | bytes 1540
  185.9 1.0 copy-start.10
  229.5 4.4 copy-start.13
  229.5 4.5 copy-start.14
  233.9 206.7 %all-gather.9.cloned.1.call-start = ((), (), s32[]{:S(2)}) async-start(), calls=%async_computation.4 | async-start | bytes 4128768 | tf_op jit(solution)/shard_map/all_gather | solution.py:116
  234.9 306.9 %reduce-scatter.4.cloned.1.call-start = ((), (), s32[]{:S(2)}) async-start(), calls=%async_computation.5 | async-start | bytes 4456448
  386.5 5.8 %copy-start.3 = (bf16[1024,2048]{1,0:T(8,128)(2,1)}, bf16[1024,2048]{1,0:T(8,128)(2,1)S(1)}, u32[]{:S(2)}) copy-start(bf16[1024,2048]{1,0:T(8,128)(2,1)S(1)} %get-tuple-element.14) | copy-start | bytes 12582916
  386.6 9.0 %collective-permute-start = (bf16[1,2048]{1,0:T(2,128)(2,1)S(1)}, bf16[1,2048]{1,0:T(2,128)(2,1)S(1)}, u32[]{:S(2)}, u32[]{:S(2)}) collective-permute-start(bf16[1,2048]{1,0:T(2,128)(2,1)S(1)} %constant_dynamic-slice_fusion.2), channel_id=1, source_target_pairs={{0,16},{16,32},{32,48},{48,64},{64,80},{80,96},{96,112},{1,17},{17... | collective-permute-start | bytes 12296 | tf_op jit(solution)/shard_map/ppermute | solution.py:18
  392.3 3.2 copy-start.5
  398.3 4.6 copy-start.4
  452.8 8.4 %copy-start.11 = (f32[7,2,64,64]{3,2,1,0:T(8,128)S(1)}, f32[7,2,64,64]{3,2,1,0:T(8,128)}, u32[]{:S(2)}) copy-start(f32[7,2,64,64]{3,2,1,0:T(8,128)} %copy-done.10) | copy-start | bytes 688132
  541.8 8.5 %copy-start.1 = (bf16[2048,160]{0,1:T(8,128)(2,1)S(1)}, bf16[2048,160]{0,1:T(8,128)(2,1)}, u32[]{:S(2)}) copy-start(bf16[2048,160]{0,1:T(8,128)(2,1)} %param.24) | copy-start | bytes 1966084
Sparse Core Ops, SparseCore 0:
  10.4 46.4 all-gather.6
  59.2 56.5 all-gather.4
  234.0 148.2 all-reduce.1
  383.8 56.7 all-gather.8
  459.4 82.2 reduce-scatter.3
where the time goes:
time: 561 us; the launch traced here: 557 us
  waiting for transfers between devices  326 us (58%)
  matrix products  72.5 us (13%)
  other arithmetic  65.3 us (12%)
  local copies, waits for them, and re-layouts  42.4 us (8%)
  blocking collectives  29 us (5%)
  between operations  18.2 us (3%)
    psum x1, waiting for transfers between devices, per_device(): lax.psum(lax.dot_general(normed, output_weight_t, (((1,), (1,)), ((), ())...  147 us
    unnamed x6, waiting for transfers between devices  77.9 us
    all_gather x1, waiting for transfers between devices, per_device(): gathered_rows = lax.all_gather(own_rows, 'head', axis=1, tiled=True)  54.3 us
    all_gather x1, waiting for transfers between devices, per_device(): second_full = lax.all_gather(second_pack, 'group', axis=1, tiled=True)  33.2 us
    all_gather x1, blocking collectives, per_device(): every_pack = lax.all_gather(leaving_pack, 'group', axis=0, tiled=False)  29 us
    dot_general x3, matrix products, mixed_inputs(): jnp.dot(column_part, blend_widening_maps[number], preferred_element_type=...  17.6 us
    all_gather x1, waiting for transfers between devices, per_device(): first_full = lax.all_gather(first_pack, 'group', axis=1, tiled=True)  13.4 us
    unnamed x57, local copies, waits for them, and re-layouts  13.2 us
  transfers between devices with their start and end apart: 6, of which 5 were waited for; matrix products, arithmetic and copies ran while one was open for 10% of the time, Pallas kernels for 0%

commit v1 on v0

--- a/solution.py
+++ b/solution.py
@@ -208,11 +208,17 @@
     page_end = page_end + page_factor[:, :, :, None] * incoming[None]
     attended = block_out.transpose(0, 2, 1, 3).reshape(slot_rows, features_on_shard)
     normed = (group_norm(attended) * attender_scaling_coefs * gating).astype(jnp.bfloat16)
-    mixer_total = lax.psum(
-        lax.dot_general(
-            normed, output_weight_t, (((1,), (1,)), ((), ())), preferred_element_type=jnp.float32
-        ).astype(jnp.bfloat16),
-        "head",
+    mixer_total = jnp.sum(
+        lax.all_gather(
+            lax.dot_general(
+                normed,
+                output_weight_t,
+                (((1,), (1,)), ((), ())),
+                preferred_element_type=jnp.float32,
+            ).astype(jnp.bfloat16),
+            "head",
+        ),
+        axis=0,
     ).astype(jnp.float32)
     residual = (embedded.astype(jnp.float32) + mixer_total).astype(jnp.bfloat16)
     last_residual = lax.dynamic_slice_in_dim(residual, live_count * PAGE - 1, 1, 0)

time: 561 us -> 746 us (1.33)
  waiting for transfers between devices: 326 us -> 486 us
  other arithmetic: 65.3 us -> 89.8 us
    all_gather x0 -> x1, waiting for transfers between devices: none -> 335 us  [per_device(): lax.all_gather(lax.dot_general(normed, output_weight_t, (((1,), (1,)), ((...]
    psum x1 -> x0, waiting for transfers between devices: 147 us -> none  [per_device(): lax.psum(lax.dot_general(normed, output_weight_t, (((1,), (1,)), ((), ())...]
    all_gather x1, waiting for transfers between devices: 33.2 us -> 5.66 us  [per_device(): second_full = lax.all_gather(second_pack, 'group', axis=1, tiled=True)]
    reduce_sum x0 -> x1, other arithmetic: none -> 24.2 us  [per_device(): jnp.sum(lax.all_gather(lax.dot_general(normed, output_weight_t, (((1,), (...]
  transfers between devices with their start and end apart: 6 -> 6, of which waited for: 5 -> 5; matrix products, arithmetic and copies ran while one was open for 10% -> 11% of each run, Pallas kernels for 0% -> 0%
where the time goes in v1:
time: 746 us; the launch traced here: 742 us
  waiting for transfers between devices  486 us (65%)
  other arithmetic  89.8 us (12%)
  matrix products  72.5 us (10%)
  local copies, waits for them, and re-layouts  42.4 us (6%)
  blocking collectives  29 us (4%)
  between operations  18.3 us (2%)
    all_gather x1, waiting for transfers between devices, per_device(): lax.all_gather(lax.dot_general(normed, output_weight_t, (((1,), (1,)), ((...  335 us
    unnamed x6, waiting for transfers between devices  77.4 us
    all_gather x1, waiting for transfers between devices, per_device(): gathered_rows = lax.all_gather(own_rows, 'head', axis=1, tiled=True)  54.3 us
    all_gather x1, blocking collectives, per_device(): every_pack = lax.all_gather(leaving_pack, 'group', axis=0, tiled=False)  29 us
    reduce_sum x1, other arithmetic, per_device(): jnp.sum(lax.all_gather(lax.dot_general(normed, output_weight_t, (((1,), (...  24.2 us
    dot_general x3, matrix products, mixed_inputs(): jnp.dot(column_part, blend_widening_maps[number], preferred_element_type=...  17.6 us
  transfers between devices with their start and end apart: 6, of which 5 were waited for; matrix products, arithmetic and copies ran while one was open for 11% of the time, Pallas kernels for 0%

profile of v1, /device:TPU:0, one launch (start us, length us, event | category | flops | bytes accessed | tf_op | source)
XLA Modules:
  0.0 741.6 jit_solution(4608810076472384271)
XLA Ops:
  8.3 1.1 convert.18
  11.2 1.3 fusion.130
  12.5 1.3 fusion.132
  13.8 1.3 gather_fusion
  15.1 1.3 compare_and_fusion.2
  16.5 1.3 maximum_bitcast_fusion
  19.4 1.3 fusion.168
  20.8 10.5 %gather_fusion.2 = bf16[1032,128]{1,0:T(8,128)(2,1)S(1)} fusion(bf16[65536,128]{1,0:T(8,128)(2,1)} %param.18, s32[2048]{0:T(1024)S(1)} %pad_clamp_fusion), kind=kCustom, calls=%fused_computation.4 | custom fusion | bytes 532512 | tf_op jit(solution)/shard_map/jit(_take)/gather | solution.py:104
  31.3 1.3 compare_select_fusion.6
  42.3 1.3 fusion.146
  43.6 13.3 %all-gather.9.cloned.1.call-done = bf16[6,2048,128]{2,1,0:T(8,128)(2,1)} async-done(((bf16[6,256,128]{2,1,0:T(8,128)(2,1)}), bf16[6,2048,128]{2,1,0:T(8,128)(2,1)}) %all-gather.9.cloned.1.call-update) | async-done | bytes 3145744 | tf_op jit(solution)/shard_map/all_gather | solution.py:115
  56.9 1.5 slice_bitcast_fusion.15
  58.4 1.1 copy.126
  61.5 54.3 %all-gather.7.cloned.1.call-done = bf16[1032,2048]{1,0:T(8,128)(2,1)} async-done(((bf16[1032,128]{1,0:T(8,128)(2,1)}), bf16[1032,2048]{1,0:T(8,128)(2,1)}) %all-gather.7.cloned.1.call-update) | async-done | bytes 4227088 | tf_op jit(solution)/shard_map/all_gather | solution.py:105
  116.8 1.2 fusion.105
  118.0 2.8 convert_reduce_fusion
  120.8 3.1 fusion.4
  124.1 1.2 fusion.2
  125.3 4.7 pad_maximum_fusion
  130.9 4.2 bitcast_subtract_fusion.1
  135.2 2.7 fusion.22
  138.4 8.0 %fusion.29 = bf16[1024,64]{0,1:T(8,128)(2,1)S(1)} fusion(bf16[2048,64]{0,1:T(8,128)(2,1)S(1)} %copy-done.18, f32[1024,2048]{1,0:T(8,128)} %copy-done.2, f32[2048]{0:T(1024)S(1)} %bitcast.331, f32[1024]{0:T(1024)S(1)} %add_rsqrt_fusion.1, f32[1024]{0:T(1024)S(1)} %broadcast_multiply_fusion.2, bf16[5,32,2048]{2,1,0:T(8,128)(2,1)} %param.25, ...), kind=kOutput, calls=%fused_computation.63 | convolution fusion | flops 417398784 | bytes 13189120 | tf_op jit(solution)/shard_map/dot_general | solution.py:48
  149.2 5.1 slice_multiply_fusion.2
  155.1 6.8 add_convert_fusion.3
  162.0 1.5 fusion.151
  163.5 7.6 %add_convert_fusion.6 = bf16[1024,2048]{1,0:T(8,128)(2,1)S(1)} fusion(f32[1024,2048]{1,0:T(8,128)} %copy-done.2, f32[2048]{0:T(1024)S(1)} %bitcast.323, f32[1024]{0:T(1024)S(1)} %add_rsqrt_fusion.1, f32[1024]{0:T(1024)S(1)} %broadcast_multiply_fusion.2, bf16[5,32,2048]{2,1,0:T(8,128)(2,1)} %param.25, bf16[1024,160]{0,1:T(8,128)(2,1)} %copy-done.15, ...), kind=kOutput, calls=%fused_computation.27 | convolution fusion | flops 148897792 | bytes 16990208 | tf_op jit(solution)/shard_map/dot_general | solution.py:37
  171.1 1.5 convolution_bitcast_fusion.4
  172.7 3.3 add_convert_fusion.4
  176.0 1.5 multiply_reduce_fusion.1
  178.6 2.3 convolution_select_fusion
  188.1 29.0 %all-gather = f32[16,65,64]{1,2,0:T(8,128)S(1)} all-gather(f32[2,65,64]{1,2,0:T(8,128)S(1)} %pad_maximum_fusion.4), channel_id=2, replica_groups=mesh['group'=8,'head'=16] {'group'}, dimensions={0}, use_global_device_ids=true | all-gather | bytes 299520 | tf_op jit(solution)/shard_map/all_gather | solution.py:197
  217.5 2.1 fusion.18
  222.2 7.5 %multiply_convert_fusion.1 = bf16[1024,128]{1,0:T(8,128)(2,1)S(1)} fusion(bf16[6,2048,128]{2,1,0:T(8,128)(2,1)} %all-gather.9.cloned.1.call-done, f32[1024,2048]{1,0:T(8,128)} %copy-done.2, f32[2048]{0:T(1024)S(1)} %bitcast.330, f32[1024]{0:T(1024)S(1)} %add_rsqrt_fusion.1, f32[1024]{0:T(1024)S(1)} %broadcast_multiply_fusion.2, f32[1024,128]{1,0:T(8,128)S(1)} %copy.137, ...), kind=kOutput, calls=%fused_computation.81 | convolution fusion | flops 686948352 | bytes 15155712 | tf_op jit(solution)/shard_map/dot_general | solution.py:136
  229.7 4.4 convolution_convert_fusion.1
  235.8 335.1 %all-gather.13.cloned.1.call-done = bf16[16384,2048]{1,0:T(8,128)(2,1)} async-done(((bf16[1024,2048]{1,0:T(8,128)(2,1)}), bf16[16384,2048]{1,0:T(8,128)(2,1)}) %all-gather.13.cloned.1.call-update) | async-done | bytes 67108880 | tf_op jit(solution)/shard_map/all_gather | solution.py:212
  570.9 24.2 %reduce_sum.138 = bf16[1024,2048]{1,0:T(8,128)(2,1)} reduce(bf16[16,1024,2048]{2,1,0:T(8,128)(2,1)} %bitcast.100, bf16[]{:T(256)} %constant.167.clone.1), dimensions={0}, to_apply=%region_13.15 | reduce | flops 31457280 | bytes 71303168 | tf_op jit(solution)/shard_map/reduce_sum | solution.py:211
  595.1 4.2 convert_reduce_fusion.1
  599.4 3.4 collective-permute-start
  602.8 1.2 fusion.5
  605.0 3.2 copy-done.5
  610.9 4.6 pad_maximum_fusion.1
  615.6 4.5 bitcast_subtract_fusion
  620.1 5.7 all-gather.11.cloned.1.call-done
  625.8 12.2 %convolution_convert_fusion = bf16[1024,2048]{1,0:T(8,128)(2,1)} fusion(bf16[2,2048,448]{1,2,0:T(8,128)(2,1)} %all-gather.11.cloned.1.call-done, f32[1024,2048]{1,0:T(8,128)} %bitcast_subtract_fusion, f32[2048]{0:T(1024)S(1)} %bitcast.329, bf16[1024,2048]{1,0:T(8,128)(2,1)} %copy-done.3, f32[1024]{0:T(1024)S(1)} %add_rsqrt_fusion, ...), kind=kOutput, calls=%fused_computation.34 | convolution fusion | flops 3774152704 | bytes 20463616 | tf_op jit(solution)/shard_map/dot_general | solution.py:242
  637.9 6.5 copy.152
  649.1 77.4 %reduce-scatter.4.cloned.1.call-done = bf16[128,1024]{1,0:T(8,128)(2,1)} async-done(((bf16[2048,1024]{1,0:T(8,128)(2,1)}), bf16[128,1024]{1,0:T(8,128)(2,1)}) %reduce-scatter.4.cloned.1.call-update) | async-done | bytes 262160
  726.4 1.2 copy.153
  727.6 7.3 fusion.30
  (173 shorter events, 40.1 us)
Async XLA Ops:
  7.2 128.0 %copy-start = (bf16[2048,160]{0,1:T(8,128)(2,1)S(1)}, bf16[2048,160]{0,1:T(8,128)(2,1)}, u32[]{:S(2)}) copy-start(bf16[2048,160]{0,1:T(8,128)(2,1)} %param.24) | copy-start | bytes 1966084
  7.2 49.7 %all-gather.9.cloned.1.call-start = ((), (), s32[]{:S(2)}) async-start(), calls=%async_computation.2 | async-start | bytes 3538944 | tf_op jit(solution)/shard_map/all_gather | solution.py:115
  10.3 105.4 %all-gather.7.cloned.1.call-start = ((), (), s32[]{:S(2)}) async-start(), calls=%async_computation.1 | async-start | bytes 4491264 | tf_op jit(solution)/shard_map/all_gather | solution.py:105
  33.7 537.2 %all-gather.13.cloned.1.call-start = ((), (), s32[]{:S(2)}) async-start(), calls=%async_computation.4 | async-start | bytes 71303168 | tf_op jit(solution)/shard_map/all_gather | solution.py:212
  115.7 8.2 %slice-start = ((s8[4227072]{0:T(1024)(128)(4,1)}), s8[4194304]{0:T(1024)(128)(4,1)S(1)}, s32[]{:S(2)}) async-start(s8[4227072]{0:T(1024)(128)(4,1)} %bitcast.297), calls=%async_computation.6 | async-start | bytes 8388608
  118.0 5.9 slice-start.1
  125.3 5.7 copy-start.6
  135.1 3.2 copy-start.2
  135.2 3.2 copy-start.18
  138.4 8.1 %copy-start.15 = (bf16[1024,160]{0,1:T(8,128)(2,1)}, bf16[1024,160]{0,1:T(8,128)(2,1)S(1)}, u32[]{:S(2)}) copy-start(bf16[1024,160]{0,1:T(8,128)(2,1)S(1)} %fusion.22) | copy-start | bytes 983044
  138.4 8.1 %copy-start.16 = (bf16[64,128]{1,0:T(8,128)(2,1)S(1)}, bf16[64,128]{1,0:T(8,128)(2,1)}, u32[]{:S(2)}) copy-start(bf16[64,128]{1,0:T(8,128)(2,1)} %param.27) | copy-start | bytes 49156
  138.4 8.1 %copy-start.17 = (f32[128]{0:T(128)S(1)}, f32[128]{0:T(128)}, u32[]{:S(2)}) copy-start(f32[128]{0:T(128)} %param.28) | copy-start | bytes 1540
  155.1 6.8 copy-start.9
  162.0 10.7 %slice-start.2 = ((s8[4227072]{0:T(1024)(128)(4,1)}), s8[4194304]{0:T(1024)(128)(4,1)S(1)}, s32[]{:S(2)}) async-start(s8[4227072]{0:T(1024)(128)(4,1)} %bitcast.299), calls=%async_computation.8 | async-start | bytes 8388608
  162.0 10.7 %slice-start.4 = ((s8[8388608]{0:T(1024)(128)(4,1)}), s8[4194304]{0:T(1024)(128)(4,1)S(1)}, s32[]{:S(2)}) async-start(s8[8388608]{0:T(1024)(128)(4,1)} %bitcast.301), calls=%async_computation.10 | async-start | bytes 8388608
  163.5 7.6 %copy-start.8 = (bf16[128,2048]{1,0:T(8,128)(2,1)S(1)}, bf16[128,2048]{1,0:T(8,128)(2,1)}, u32[]{:S(2)}) copy-start(bf16[128,2048]{1,0:T(8,128)(2,1)} %copy.121) | copy-start | bytes 1572868
  163.5 9.1 %slice-start.3 = ((s8[4227072]{0:T(1024)(128)(4,1)}), s8[32768]{0:T(1024)(128)(4,1)S(1)}, s32[]{:S(2)}) async-start(s8[4227072]{0:T(1024)(128)(4,1)} %bitcast.299), calls=%async_computation.9 | async-start | bytes 65536
  163.5 9.1 %slice-start.5 = ((s8[8388608]{0:T(1024)(128)(4,1)}), s8[4194304]{0:T(1024)(128)(4,1)S(1)}, s32[]{:S(2)}) async-start(s8[8388608]{0:T(1024)(128)(4,1)} %bitcast.301), calls=%async_computation.11 | async-start | bytes 8388608
  172.7 3.3 copy-start.7
  176.0 4.9 copy-start.12
  182.4 39.9 %copy-start.19 = (f32[128]{0:T(128)S(1)}, f32[128]{0:T(128)}, u32[]{:S(2)}) copy-start(f32[128]{0:T(128)} %param.30) | copy-start | bytes 1540
  186.0 1.0 copy-start.10
  229.7 4.5 copy-start.13
  229.7 4.5 copy-start.14
  234.1 391.7 %all-gather.11.cloned.1.call-start = ((), (), s32[]{:S(2)}) async-start(), calls=%async_computation.3 | async-start | bytes 4128768 | tf_op jit(solution)/shard_map/all_gather | solution.py:116
  235.1 491.3 %reduce-scatter.4.cloned.1.call-start = ((), (), s32[]{:S(2)}) async-start(), calls=%async_computation.5 | async-start | bytes 4456448
  599.3 5.6 copy-start.3
  599.4 8.8 %collective-permute-start = (bf16[1,2048]{1,0:T(2,128)(2,1)S(1)}, bf16[1,2048]{1,0:T(2,128)(2,1)S(1)}, u32[]{:S(2)}, u32[]{:S(2)}) collective-permute-start(bf16[1,2048]{1,0:T(2,128)(2,1)S(1)} %constant_dynamic-slice_fusion.2), channel_id=1, source_target_pairs={{0,16},{16,32},{32,48},{48,64},{64,80},{80,96},{96,112},{1,17},{17... | collective-permute-start | bytes 12296 | tf_op jit(solution)/shard_map/ppermute | solution.py:18
  604.9 3.2 copy-start.5
  610.9 4.7 copy-start.4
  637.9 8.4 %copy-start.11 = (f32[7,2,64,64]{3,2,1,0:T(8,128)S(1)}, f32[7,2,64,64]{3,2,1,0:T(8,128)}, u32[]{:S(2)}) copy-start(f32[7,2,64,64]{3,2,1,0:T(8,128)} %copy-done.10) | copy-start | bytes 688132
  726.4 8.5 %copy-start.1 = (bf16[2048,160]{0,1:T(8,128)(2,1)S(1)}, bf16[2048,160]{0,1:T(8,128)(2,1)}, u32[]{:S(2)}) copy-start(bf16[2048,160]{0,1:T(8,128)(2,1)} %param.24) | copy-start | bytes 1966084
Sparse Core Ops, SparseCore 0:
  10.4 46.4 all-gather.8
  59.2 56.4 all-gather.6
  234.2 336.6 all-gather.12
  572.3 53.3 all-gather.10
  644.5 81.8 reduce-scatter.3
